TPU v7x, 32 devices: a whole 2x2x4 slice. The times are simulated.
32 devices in a mesh: slab: 8 (over z, y), coil: 4 (over x, core).
Axes of the slice: x: 2, y: 2, z: 4, core: 2. Of those that a mesh axis runs over, the one named last changes fastest.
Arguments:
- image: bfloat16 [2, 320, 256, 128], P(None, None, 'slab'), may hold values from -6 to 6
- coil_maps: bfloat16 [16, 320, 256, 128], P('coil', None, 'slab'), may hold values from -5 to 5
- y_data: bfloat16 [2, 16, 320, 128, 128], P(None, 'coil', 'slab'), may hold values from -6 to 6
- kz_lines: int32 [2, 320, 128], P(None, 'slab'), may hold values from -1 to 255, as said below
Outputs:
- gradient: bfloat16 [2, 320, 256, 128], P(None, 'coil', 'slab')
Inputs may be any that keep to these rules, and one draw needn't show every extreme that they name: kz_lines[m, ky, :] lists distinct sampled kz of that ky row first and -1 in the unused slots after them; every row has at least one sampled kz; row 160 uses all 128 slots.
All inputs are finite; a program needn't handle non-finite values.
Results may differ from a plain program's by a relative error of at most 0.0061.
Values may be sent and summed in bfloat16 or wider, within the bound.
No kernel may reach another device: no remote copies, remote signals or barrier semaphores. Data moves between devices by JAX's collectives and lax.ppermute only.
A program may use at most 256 MiB of HBM per device.

v0:
```python
import math
import jax
import jax.numpy as jnp
from jax import lax
from jax.sharding import PartitionSpec as P


def cos_sin(length):
    positions = jnp.arange(length, dtype=jnp.int32)
    phase = (positions[:, None] * positions[None, :] % length).astype(jnp.float32) * (
        2.0 * math.pi / length
    )
    factor = 1.0 / math.sqrt(length)
    return (
        (jnp.cos(phase) * factor).astype(jnp.bfloat16),
        (jnp.sin(phase) * factor).astype(jnp.bfloat16),
    )


def lane_tables(lane_count):
    half_lanes = lane_count // 2
    rows = jnp.arange(lane_count, dtype=jnp.int32)[:, None]
    cols = jnp.arange(lane_count, dtype=jnp.int32)[None, :]
    rotate = jnp.where((rows == cols + half_lanes) & (cols < half_lanes), -1.0, 0.0)
    rotate = rotate + jnp.where((cols == rows + half_lanes) & (rows < half_lanes), 1.0, 0.0)
    same_slot = rows % half_lanes == cols % half_lanes
    dup_real = jnp.where(same_slot & (rows < half_lanes), 1.0, 0.0)
    dup_imag = jnp.where(same_slot & (rows >= half_lanes), 1.0, 0.0)
    return (
        rotate.astype(jnp.bfloat16),
        dup_real.astype(jnp.bfloat16),
        dup_imag.astype(jnp.bfloat16),
    )


def lane_map(values, table):
    if values.dtype == jnp.bfloat16:
        return jnp.einsum("...l,lm->...m", values, table, preferred_element_type=jnp.float32)
    return jnp.einsum(
        "...l,lm->...m", values, table.astype(jnp.float32), precision=lax.Precision.HIGHEST
    )


def transform(image, coil_maps, y_data, kz_lines, forward, backward):
    state_count, y_count, z_local, lane_count = image.shape
    rotate, dup_real, dup_imag = lane_tables(lane_count)
    y_cos, y_sin = cos_sin(y_count)
    sens_real = lane_map(coil_maps, dup_real)[None]
    sens_imag = lane_map(coil_maps, dup_imag)[None]
    pixels = image.astype(jnp.float32)[:, None]
    turned_pixels = lane_map(image, rotate)[:, None]
    coil_image = (sens_real * pixels + sens_imag * turned_pixels).astype(jnp.bfloat16)
    turned_image = lane_map(coil_image, rotate).astype(jnp.bfloat16)
    spectrum = (
        jnp.einsum("ky,scyzl->sckzl", y_cos, coil_image, preferred_element_type=jnp.float32)
        - jnp.einsum("ky,scyzl->sckzl", y_sin, turned_image, preferred_element_type=jnp.float32)
    ).astype(jnp.bfloat16)
    gathered = forward(spectrum)
    z_count = gathered.shape[3]
    z_cos, z_sin = cos_sin(z_count)
    turned_gathered = lane_map(gathered, rotate).astype(jnp.bfloat16)
    sampled = kz_lines >= 0
    kz_index = jnp.maximum(kz_lines, 0)
    onehot = (
        (kz_index[..., None] == jnp.arange(z_count, dtype=jnp.int32)) & sampled[..., None]
    ).astype(jnp.bfloat16)
    measured = y_data.astype(jnp.float32)
    sampled_wide = sampled[:, None, :, :, None]
    kspace = jnp.einsum(
        "jq,sckql->sckjl", z_cos, gathered, preferred_element_type=jnp.float32
    ) - jnp.einsum("jq,sckql->sckjl", z_sin, turned_gathered, preferred_element_type=jnp.float32)
    picked = jnp.einsum(
        "skjq,sckql->sckjl", onehot.astype(jnp.float32), kspace, precision=lax.Precision.HIGHEST
    )
    residual = jnp.where(sampled_wide, picked - measured, jnp.float32(0.0)).astype(jnp.bfloat16)
    kz_grid = jnp.einsum(
        "skjq,sckjl->sckql", onehot, residual, preferred_element_type=jnp.float32
    ).astype(jnp.bfloat16)
    turned_grid = lane_map(kz_grid, rotate).astype(jnp.bfloat16)
    adjoint_z = (
        jnp.einsum("qz,sckql->sckzl", z_cos, kz_grid, preferred_element_type=jnp.float32)
        + jnp.einsum("qz,sckql->sckzl", z_sin, turned_grid, preferred_element_type=jnp.float32)
    ).astype(jnp.bfloat16)
    returned = backward(adjoint_z)
    turned_returned = lane_map(returned, rotate).astype(jnp.bfloat16)
    coil_back = jnp.einsum(
        "ky,sckzl->scyzl", y_cos, returned, preferred_element_type=jnp.float32
    ) + jnp.einsum("ky,sckzl->scyzl", y_sin, turned_returned, preferred_element_type=jnp.float32)
    turned_back = lane_map(coil_back, rotate)
    return jnp.sum(sens_real * coil_back - sens_imag * turned_back, axis=1)


def shards(image, coil_maps, y_data, kz_lines):
    partial_image = transform(
        image,
        coil_maps,
        y_data,
        kz_lines,
        lambda payload: lax.all_to_all(payload, "slab", split_axis=2, concat_axis=3, tiled=True),
        lambda payload: lax.all_to_all(payload, "slab", split_axis=3, concat_axis=2, tiled=True),
    )
    summed = lax.psum(partial_image, "coil")
    portion = summed.shape[1] // lax.axis_size("coil")
    summed = lax.dynamic_slice_in_dim(summed, lax.axis_index("coil") * portion, portion, 1)
    return summed.astype(jnp.bfloat16)


def solution(mesh):
    in_specs = (
        P(None, None, "slab", None),
        P("coil", None, "slab", None),
        P(None, "coil", "slab", None, None),
        P(None, "slab", None),
    )
    out_specs = P(None, "coil", "slab", None)
    return jax.shard_map(shards, mesh=mesh, in_specs=in_specs, out_specs=out_specs, check_vma=False)
```

profile of v0, /device:TPU:1, one launch (start us, length us, event | category | flops | bytes accessed | tf_op | source)
XLA Modules:
  0.0 1599.3 jit_solution(7993726364527364379)
XLA Ops:
  0.0 0.0 slice-start
  0.0 2.0 fusion.257
  2.0 0.0 slice-start.1
  2.0 8.3 copy.50
  10.4 0.0 slice-start.2
  10.4 8.6 fusion.72
  19.0 0.0 slice-done
  19.0 0.0 slice-done.1
  19.0 0.0 slice-done.2
  19.0 9.1 fusion.56
  28.1 9.1 fusion.59
  37.2 44.6 %fusion.8 = f32[2,4,32,128,320]{3,4,2,1,0:T(8,128)} fusion(f32[2,320,32,128]{3,1,2,0:T(8,128)} %fusion.72, f32[4,320,32,128]{3,1,2,0:T(8,128)} %fusion.59, f32[2,320,32,128]{3,1,2,0:T(8,128)} %copy.50, f32[4,320,32,128]{3,1,2,0:T(8,128)} %fusion.56), kind=kOutput, calls=%fused_computation.12 | convolution fusion | flops 6753955840 | bytes 104857600 | tf_op jit(solution)/shard_map/ky,scyzl->sckzl/dot_general | solution.py:55
  81.8 43.1 %fusion.9 = bf16[2,4,320,32,128]{4,2,3,1,0:T(8,128)(2,1)} fusion(f32[2,4,32,128,320]{3,4,2,1,0:T(8,128)} %fusion.8, f32[2,320,32,128]{3,1,2,0:T(8,128)} %fusion.72, f32[4,320,32,128]{3,1,2,0:T(8,128)} %fusion.59, f32[2,320,32,128]{3,1,2,0:T(8,128)} %copy.50, f32[4,320,32,128]{3,1,2,0:T(8,128)} %fusion.56, s32[128]{0:T(128)S(1)} %iota_add_fusion, ...), kind=kOutput, calls=%fused_computation.13 | convolution fusion | flops 9468772352 | bytes 126034560 | tf_op jit(solution)/shard_map/ky,scyzl->sckzl/dot_general | solution.py:56
  124.9 21.4 %copy.55 = bf16[2,4,320,32,128]{4,3,1,0,2:T(8,128)(2,1)} copy(bf16[2,4,320,32,128]{4,2,3,1,0:T(8,128)(2,1)} %fusion.9) | data formatting | bytes 41943040 | tf_op jit(solution)/shard_map/convert_element_type | solution.py:57
  146.3 6.8 all-to-all-start
  153.2 0.0 copy-start
  153.2 13.7 copy.60
  166.9 1.0 fusion.263
  167.9 1.0 fusion.261
  168.9 0.0 copy-done
  169.0 437.4 %all-to-all-done = bf16[2,4,320,32,128]{4,3,1,0,2:T(8,128)(2,1)} async-done(((bf16[2,4,320,32,128]{4,3,1,0,2:T(8,128)(2,1)}), bf16[2,4,320,32,128]{4,3,1,0,2:T(8,128)(2,1)}, u32[]{:S(2)}, u32[]{:S(2)}) %all-to-all-start) | async-done | bytes 20971552 | tf_op jit(solution)/shard_map/all_to_all | solution.py:99
  606.3 19.2 %copy.57 = bf16[2,4,40,8,32,128]{5,4,3,2,1,0:T(8,128)(2,1)} copy(bf16[2,4,40,8,32,128]{5,4,1,0,2,3:T(8,128)(2,1)} %bitcast.16) | data formatting | bytes 41943040 | tf_op jit(solution)/shard_map/all_to_all | solution.py:99
  625.5 21.7 %fusion.98 = f32[2,4,40,128,256]{4,3,2,1,0:T(8,128)} fusion(bf16[2,4,40,256,128]{4,3,2,1,0:T(8,128)(2,1)} %bitcast.172), kind=kOutput, calls=%fused_computation.86 | convolution fusion | flops 5369757696 | bytes 62914560 | tf_op jit(solution)/shard_map/jq,sckql->sckjl/dot_general | solution.py:69
  647.3 24.3 %fusion.21 = f32[2,4,40,128,256]{4,3,2,1,0:T(8,128)} fusion(bf16[2,4,40,256,128]{4,3,2,1,0:T(8,128)(2,1)} %bitcast.173, s32[128]{0:T(128)S(1)} %iota_add_fusion, pred[128]{0:T(512)(128)(4,1)S(1)} %iota_compare_fusion.4, bf16[256,256,1,1,1]{1,0,4,3,2:T(8,128)(2,1)S(1)} %fusion.263), kind=kOutput, calls=%fused_computation.25 | convolution fusion | flops 8063680512 | bytes 63046272 | tf_op jit(solution)/shard_map/jq,sckql->sckjl/dot_general | solution.py:71
  671.6 38.0 %fusion.12 = bf16[2,4,40,128,128]{3,4,2,1,0:T(8,128)(2,1)} fusion(bf16[2,4,40,128,128]{3,4,2,1,0:T(8,128)(2,1)} %copy.60, pred[2,40,128]{2,1,0:T(8,128)(4,1)S(1)} %broadcast_compare_fusion, f32[2,4,40,128,256]{4,3,2,1,0:T(8,128)} %fusion.98, f32[2,4,40,128,256]{4,3,2,1,0:T(8,128)} %fusion.21, s32[2,40,128]{2,1,0:T(8,128)S(1)} %broadcast_maximum_fusion), kind=kOutput, calls=%fused_computation.17 | convolution fusion | flops 16142827520 | bytes 104908800 | tf_op jit(solution)/shard_map/skjq,sckql->sckjl/dot_general | solution.py:72
  709.6 13.7 convert_bitcast_fusion
  723.2 28.2 %fusion.17 = f32[2,4,40,128,256]{4,3,2,1,0:T(8,128)} fusion(bf16[2,4,40,256,128]{3,4,1,2,0:T(8,128)(2,1)} %convert_bitcast_fusion, s32[128]{0:T(128)S(1)} %iota_add_fusion, pred[128]{0:T(512)(128)(4,1)S(1)} %iota_compare_fusion.4, bf16[256,256,1,1,1]{1,0,4,3,2:T(8,128)(2,1)S(1)} %fusion.261), kind=kOutput, calls=%fused_computation.21 | convolution fusion | flops 8063680512 | bytes 63046272 | tf_op jit(solution)/shard_map/qz,sckql->sckzl/dot_general | solution.py:82
  751.5 29.8 %fusion.10 = bf16[2,4,40,256,128]{3,4,2,1,0:T(8,128)(2,1)} fusion(f32[2,4,40,128,256]{4,3,2,1,0:T(8,128)} %fusion.17, bf16[2,4,40,256,128]{3,4,1,2,0:T(8,128)(2,1)} %convert_bitcast_fusion), kind=kOutput, calls=%fused_computation.14 | convolution fusion | flops 5390729216 | bytes 83886080 | tf_op jit(solution)/shard_map/qz,sckql->sckzl/dot_general | solution.py:81
  781.3 30.6 %copy.65 = bf16[2,4,40,256,128]{4,2,1,0,3:T(8,128)(2,1)} copy(bf16[2,4,40,256,128]{3,4,2,1,0:T(8,128)(2,1)} %fusion.10) | data formatting | bytes 41943040 | tf_op jit(solution)/shard_map/convert_element_type | solution.py:83
  811.9 6.1 all-to-all-start.1
  818.1 2.0 fusion.259
  820.0 449.4 %all-to-all-done.1 = bf16[2,4,40,256,128]{4,2,1,0,3:T(8,128)(2,1)} async-done(((bf16[2,4,40,256,128]{4,2,1,0,3:T(8,128)(2,1)}), bf16[2,4,40,256,128]{4,2,1,0,3:T(8,128)(2,1)}, u32[]{:S(2)}, u32[]{:S(2)}) %all-to-all-start.1) | async-done | bytes 20971552 | tf_op jit(solution)/shard_map/all_to_all | solution.py:100
  1269.5 19.4 %copy.67 = bf16[2,4,8,40,32,128]{5,3,2,4,1,0:T(8,128)(2,1)} copy(bf16[2,4,8,40,32,128]{5,3,1,0,4,2:T(8,128)(2,1)} %bitcast.33) | data formatting | bytes 41943040 | tf_op jit(solution)/shard_map/all_to_all | solution.py:100
  1288.9 26.3 %fusion.90 = f32[2,4,32,128,320]{3,4,2,1,0:T(8,128)} fusion(bf16[2,4,320,32,128]{4,2,3,1,0:T(8,128)(2,1)} %bitcast.170), kind=kOutput, calls=%fused_computation.83 | convolution fusion | flops 6712012800 | bytes 62914560 | tf_op jit(solution)/shard_map/ky,sckzl->scyzl/dot_general | solution.py:86
  1315.2 27.4 %fusion.13 = f32[2,4,32,128,320]{3,4,2,1,0:T(8,128)} fusion(bf16[2,4,320,32,128]{4,2,3,1,0:T(8,128)(2,1)} %bitcast.171, s32[128]{0:T(128)S(1)} %iota_add_fusion, pred[128]{0:T(512)(128)(4,1)S(1)} %iota_compare_fusion.4, bf16[320,320,1,1,1]{0,1,4,3,2:T(8,128)(2,1)S(1)} %fusion.259), kind=kOutput, calls=%fused_computation.18 | convolution fusion | flops 9405857792 | bytes 63120000 | tf_op jit(solution)/shard_map/ky,sckzl->scyzl/dot_general | solution.py:88
  1342.6 69.9 %fusion.3 = f32[2,320,32,128]{3,1,2,0:T(8,128)} fusion(f32[4,320,32,128]{3,1,2,0:T(8,128)} %fusion.59, f32[4,320,32,128]{3,1,2,0:T(8,128)} %fusion.56, f32[2,4,32,128,320]{3,4,2,1,0:T(8,128)} %fusion.90, f32[2,4,32,128,320]{3,4,2,1,0:T(8,128)} %fusion.13, s32[128]{0:T(128)S(1)} %iota_add_fusion, pred[128]{0:T(512)(128)(4,1)S(1)} %iota_compare_fusion.4), kind=kOutput, calls=%fused_computation.4 | convolution fusion | flops 16166551552 | bytes 136315520 | tf_op jit(solution)/shard_map/...l,lm->...m/dot_general | solution.py:39
  1412.5 183.5 %all-reduce.1 = bf16[2,320,32,128]{3,1,2,0:T(8,128)(2,1)} all-reduce(f32[2,320,32,128]{3,1,2,0:T(8,128)} %fusion.3), channel_id=1, replica_groups=mesh['slab'=8,'coil'=4] {'coil'}, use_global_device_ids=true, to_apply=%region_1.2 | all-reduce | flops 2621440 | bytes 15728640 | tf_op jit(solution)/shard_map/psum | solution.py:102
  1596.1 1.4 dynamic-slice_convert_fusion
  1597.5 1.4 copy.70
  (7 shorter events, 0.0 us)
Async XLA Ops:
  0.0 19.0 %slice-start = ((s8[10485760]{0:T(1024)(128)(4,1)}), s8[4194304]{0:T(1024)(128)(4,1)S(1)}, s32[]{:S(2)}) async-start(s8[10485760]{0:T(1024)(128)(4,1)} %bitcast.174), calls=%async_computation.2 | async-start | bytes 8388608
  2.0 17.0 %slice-start.1 = ((s8[10485760]{0:T(1024)(128)(4,1)}), s8[4194304]{0:T(1024)(128)(4,1)S(1)}, s32[]{:S(2)}) async-start(s8[10485760]{0:T(1024)(128)(4,1)} %bitcast.174), calls=%async_computation.3 | async-start | bytes 8388608
  10.4 8.6 slice-start.2
  146.3 460.0 %all-to-all-start = ((bf16[2,4,320,32,128]{4,3,1,0,2:T(8,128)(2,1)}), bf16[2,4,320,32,128]{4,3,1,0,2:T(8,128)(2,1)}, u32[]{:S(2)}, u32[]{:S(2)}) async-start(bf16[2,4,320,32,128]{4,3,1,0,2:T(8,128)(2,1)} %copy.55), calls=%async_computation | async-start | bytes 41943040 | tf_op jit(solution)/shard_map/all_to_all | solution.py:99
  153.2 15.7 copy-start
  811.9 457.5 %all-to-all-start.1 = ((bf16[2,4,40,256,128]{4,2,1,0,3:T(8,128)(2,1)}), bf16[2,4,40,256,128]{4,2,1,0,3:T(8,128)(2,1)}, u32[]{:S(2)}, u32[]{:S(2)}) async-start(bf16[2,4,40,256,128]{4,2,1,0,3:T(8,128)(2,1)} %copy.65), calls=%async_computation.1 | async-start | bytes 41943040 | tf_op jit(solution)/shard_map/all_to_all | solution.py:100
where the time goes:
time: 1610 us; the launch traced here: 1600 us
  waiting for transfers between devices  887 us (55%)
  matrix products  394 us (24%)
  blocking collectives  184 us (11%)
  local copies, waits for them, and re-layouts  116 us (7%)
    all_to_all x1, waiting for transfers between devices, shards(): lax.all_to_all(payload, 'slab', split_axis=3, concat_axis=2, tiled=True)  449 us
    all_to_all x1, waiting for transfers between devices, shards(): lax.all_to_all(payload, 'slab', split_axis=2, concat_axis=3, tiled=True)  437 us
    psum x1, blocking collectives, shards(): summed = lax.psum(partial_image, 'coil')  184 us
    dot_general x1, matrix products, lane_map(): jnp.einsum('...l,lm->...m', values, table.astype(jnp.float32), precision=...  69.9 us
    dot_general x1, matrix products, transform(): jnp.einsum('ky,scyzl->sckzl', y_cos, coil_image, preferred_element_type=j...  44.6 us
    dot_general x1, matrix products, transform(): jnp.einsum('ky,scyzl->sckzl', y_sin, turned_image, preferred_element_type...  43.1 us
    dot_general x1, matrix products, transform(): jnp.einsum('skjq,sckql->sckjl', onehot.astype(jnp.float32), kspace, preci...  38 us
  transfers between devices with their start and end apart: 2, of which 2 were waited for; matrix products, arithmetic and copies ran while one was open for 1% of the time, Pallas kernels for 0%

commit v1 on v0

--- a/solution.py
+++ b/solution.py
@@ -99,7 +99,7 @@
         lambda payload: lax.all_to_all(payload, "slab", split_axis=2, concat_axis=3, tiled=True),
         lambda payload: lax.all_to_all(payload, "slab", split_axis=3, concat_axis=2, tiled=True),
     )
-    summed = lax.psum(partial_image, "coil")
+    summed = jnp.sum(lax.all_gather(partial_image, "coil"), axis=0)
     portion = summed.shape[1] // lax.axis_size("coil")
     summed = lax.dynamic_slice_in_dim(summed, lax.axis_index("coil") * portion, portion, 1)
     return summed.astype(jnp.bfloat16)

time: 1610 us -> 1720 us (1.068)
  waiting for transfers between devices: 887 us -> 1140 us
  blocking collectives: 184 us -> 0 us
  other arithmetic: 5.94 us -> 25.4 us
    all_gather x0 -> x1, waiting for transfers between devices: none -> 251 us  [shards(): summed = jnp.sum(lax.all_gather(partial_image, 'coil'), axis=0)]
    psum x1 -> x0, blocking collectives: 184 us -> none  [shards(): summed = lax.psum(partial_image, 'coil')]
    reduce_sum x0 -> x1, other arithmetic: none -> 19.5 us  [shards(): summed = jnp.sum(lax.all_gather(partial_image, 'coil'), axis=0)]
  transfers between devices with their start and end apart: 2 -> 3, of which waited for: 2 -> 3; matrix products, arithmetic and copies ran while one was open for 1% -> 1% of each run, Pallas kernels for 0% -> 0%
where the time goes in v1:
time: 1720 us
  waiting for transfers between devices  1140 us (66%)
  matrix products  394 us (23%)
  local copies, waits for them, and re-layouts  131 us (8%)
  other arithmetic  25.4 us (1%)
    all_to_all x1, waiting for transfers between devices, shards(): lax.all_to_all(payload, 'slab', split_axis=3, concat_axis=2, tiled=True)  449 us
    all_to_all x1, waiting for transfers between devices, shards(): lax.all_to_all(payload, 'slab', split_axis=2, concat_axis=3, tiled=True)  437 us
    all_gather x1, waiting for transfers between devices, shards(): summed = jnp.sum(lax.all_gather(partial_image, 'coil'), axis=0)  251 us
    dot_general x1, matrix products, lane_map(): jnp.einsum('...l,lm->...m', values, table.astype(jnp.float32), precision=...  69.9 us
    dot_general x1, matrix products, transform(): jnp.einsum('ky,scyzl->sckzl', y_cos, coil_image, preferred_element_type=j...  44.6 us
    dot_general x1, matrix products, transform(): jnp.einsum('ky,scyzl->sckzl', y_sin, turned_image, preferred_element_type...  43.1 us
    dot_general x1, matrix products, transform(): jnp.einsum('skjq,sckql->sckjl', onehot.astype(jnp.float32), kspace, preci...  38 us
  transfers between devices with their start and end apart: 3, of which 3 were waited for; matrix products, arithmetic and copies ran while one was open for 1% of the time, Pallas kernels for 0%

profile of v1, /device:TPU:1, one launch (start us, length us, event | category | flops | bytes accessed | tf_op | source)
XLA Modules:
  0.0 1715.8 jit_solution(12390046690667672285)
XLA Ops:
  6.5 0.0 slice-start
  6.6 2.0 fusion.257
  8.5 0.0 slice-start.1
  8.5 8.3 copy.50
  16.9 0.0 slice-start.2
  16.9 8.6 fusion.72
  25.5 0.0 slice-done
  25.5 0.0 slice-done.1
  25.5 0.0 slice-done.2
  25.5 9.1 fusion.56
  34.6 9.1 fusion.59
  43.7 44.6 %fusion.8 = f32[2,4,32,128,320]{3,4,2,1,0:T(8,128)} fusion(f32[2,320,32,128]{3,1,2,0:T(8,128)} %fusion.72, f32[4,320,32,128]{3,1,2,0:T(8,128)} %fusion.59, f32[2,320,32,128]{3,1,2,0:T(8,128)} %copy.50, f32[4,320,32,128]{3,1,2,0:T(8,128)} %fusion.56), kind=kOutput, calls=%fused_computation.12 | convolution fusion | flops 6753955840 | bytes 104857600 | tf_op jit(solution)/shard_map/ky,scyzl->sckzl/dot_general | solution.py:55
  88.3 43.1 %fusion.9 = bf16[2,4,320,32,128]{4,2,3,1,0:T(8,128)(2,1)} fusion(f32[2,4,32,128,320]{3,4,2,1,0:T(8,128)} %fusion.8, f32[2,320,32,128]{3,1,2,0:T(8,128)} %fusion.72, f32[4,320,32,128]{3,1,2,0:T(8,128)} %fusion.59, f32[2,320,32,128]{3,1,2,0:T(8,128)} %copy.50, f32[4,320,32,128]{3,1,2,0:T(8,128)} %fusion.56, s32[128]{0:T(128)S(1)} %iota_add_fusion, ...), kind=kOutput, calls=%fused_computation.13 | convolution fusion | flops 9468772352 | bytes 126034560 | tf_op jit(solution)/shard_map/ky,scyzl->sckzl/dot_general | solution.py:56
  131.5 21.4 %copy.55 = bf16[2,4,320,32,128]{4,3,1,0,2:T(8,128)(2,1)} copy(bf16[2,4,320,32,128]{4,2,3,1,0:T(8,128)(2,1)} %fusion.9) | data formatting | bytes 41943040 | tf_op jit(solution)/shard_map/convert_element_type | solution.py:57
  152.9 6.8 all-to-all-start
  159.7 0.0 copy-start
  159.7 13.8 copy.60
  173.6 1.0 fusion.263
  174.6 1.0 fusion.261
  175.5 0.0 copy-done
  175.6 437.3 %all-to-all-done = bf16[2,4,320,32,128]{4,3,1,0,2:T(8,128)(2,1)} async-done(((bf16[2,4,320,32,128]{4,3,1,0,2:T(8,128)(2,1)}), bf16[2,4,320,32,128]{4,3,1,0,2:T(8,128)(2,1)}, u32[]{:S(2)}, u32[]{:S(2)}) %all-to-all-start) | async-done | bytes 20971552 | tf_op jit(solution)/shard_map/all_to_all | solution.py:99
  612.9 19.2 %copy.57 = bf16[2,4,40,8,32,128]{5,4,3,2,1,0:T(8,128)(2,1)} copy(bf16[2,4,40,8,32,128]{5,4,1,0,2,3:T(8,128)(2,1)} %bitcast.16) | data formatting | bytes 41943040 | tf_op jit(solution)/shard_map/all_to_all | solution.py:99
  632.2 21.7 %fusion.98 = f32[2,4,40,128,256]{4,3,2,1,0:T(8,128)} fusion(bf16[2,4,40,256,128]{4,3,2,1,0:T(8,128)(2,1)} %bitcast.173), kind=kOutput, calls=%fused_computation.86 | convolution fusion | flops 5369757696 | bytes 62914560 | tf_op jit(solution)/shard_map/jq,sckql->sckjl/dot_general | solution.py:69
  653.9 24.3 %fusion.21 = f32[2,4,40,128,256]{4,3,2,1,0:T(8,128)} fusion(bf16[2,4,40,256,128]{4,3,2,1,0:T(8,128)(2,1)} %bitcast.174, s32[128]{0:T(128)S(1)} %iota_add_fusion, pred[128]{0:T(512)(128)(4,1)S(1)} %iota_compare_fusion.4, bf16[256,256,1,1,1]{1,0,4,3,2:T(8,128)(2,1)S(1)} %fusion.263), kind=kOutput, calls=%fused_computation.25 | convolution fusion | flops 8063680512 | bytes 63046272 | tf_op jit(solution)/shard_map/jq,sckql->sckjl/dot_general | solution.py:71
  678.2 38.0 %fusion.12 = bf16[2,4,40,128,128]{3,4,2,1,0:T(8,128)(2,1)} fusion(bf16[2,4,40,128,128]{3,4,2,1,0:T(8,128)(2,1)} %copy.60, pred[2,40,128]{2,1,0:T(8,128)(4,1)S(1)} %broadcast_compare_fusion, f32[2,4,40,128,256]{4,3,2,1,0:T(8,128)} %fusion.98, f32[2,4,40,128,256]{4,3,2,1,0:T(8,128)} %fusion.21, s32[2,40,128]{2,1,0:T(8,128)S(1)} %broadcast_maximum_fusion), kind=kOutput, calls=%fused_computation.17 | convolution fusion | flops 16142827520 | bytes 104908800 | tf_op jit(solution)/shard_map/skjq,sckql->sckjl/dot_general | solution.py:72
  716.2 13.6 convert_bitcast_fusion
  729.9 28.2 %fusion.17 = f32[2,4,40,128,256]{4,3,2,1,0:T(8,128)} fusion(bf16[2,4,40,256,128]{3,4,1,2,0:T(8,128)(2,1)} %convert_bitcast_fusion, s32[128]{0:T(128)S(1)} %iota_add_fusion, pred[128]{0:T(512)(128)(4,1)S(1)} %iota_compare_fusion.4, bf16[256,256,1,1,1]{1,0,4,3,2:T(8,128)(2,1)S(1)} %fusion.261), kind=kOutput, calls=%fused_computation.21 | convolution fusion | flops 8063680512 | bytes 63046272 | tf_op jit(solution)/shard_map/qz,sckql->sckzl/dot_general | solution.py:82
  758.1 29.8 %fusion.10 = bf16[2,4,40,256,128]{3,4,2,1,0:T(8,128)(2,1)} fusion(f32[2,4,40,128,256]{4,3,2,1,0:T(8,128)} %fusion.17, bf16[2,4,40,256,128]{3,4,1,2,0:T(8,128)(2,1)} %convert_bitcast_fusion), kind=kOutput, calls=%fused_computation.14 | convolution fusion | flops 5390729216 | bytes 83886080 | tf_op jit(solution)/shard_map/qz,sckql->sckzl/dot_general | solution.py:81
  787.9 32.6 %copy.65 = bf16[2,4,40,256,128]{4,2,1,0,3:T(8,128)(2,1)} copy(bf16[2,4,40,256,128]{3,4,2,1,0:T(8,128)(2,1)} %fusion.10) | data formatting | bytes 41943040 | tf_op jit(solution)/shard_map/convert_element_type | solution.py:83
  820.5 6.1 all-to-all-start.1
  826.6 0.0 all-gather.3.cloned.1.call-start
  826.7 2.0 fusion.259
  828.6 449.4 %all-to-all-done.1 = bf16[2,4,40,256,128]{4,2,1,0,3:T(8,128)(2,1)} async-done(((bf16[2,4,40,256,128]{4,2,1,0,3:T(8,128)(2,1)}), bf16[2,4,40,256,128]{4,2,1,0,3:T(8,128)(2,1)}, u32[]{:S(2)}, u32[]{:S(2)}) %all-to-all-start.1) | async-done | bytes 20971552 | tf_op jit(solution)/shard_map/all_to_all | solution.py:100
  1278.1 19.4 %copy.67 = bf16[2,4,8,40,32,128]{5,3,2,4,1,0:T(8,128)(2,1)} copy(bf16[2,4,8,40,32,128]{5,3,1,0,4,2:T(8,128)(2,1)} %bitcast.33) | data formatting | bytes 41943040 | tf_op jit(solution)/shard_map/all_to_all | solution.py:100
  1297.5 26.6 %fusion.90 = f32[2,4,32,128,320]{3,4,2,1,0:T(8,128)} fusion(bf16[2,4,320,32,128]{4,2,3,1,0:T(8,128)(2,1)} %bitcast.171), kind=kOutput, calls=%fused_computation.83 | convolution fusion | flops 6712012800 | bytes 62914560 | tf_op jit(solution)/shard_map/ky,sckzl->scyzl/dot_general | solution.py:86
  1324.1 27.4 %fusion.13 = f32[2,4,32,128,320]{3,4,2,1,0:T(8,128)} fusion(bf16[2,4,320,32,128]{4,2,3,1,0:T(8,128)(2,1)} %bitcast.172, s32[128]{0:T(128)S(1)} %iota_add_fusion, pred[128]{0:T(512)(128)(4,1)S(1)} %iota_compare_fusion.4, bf16[320,320,1,1,1]{0,1,4,3,2:T(8,128)(2,1)S(1)} %fusion.259), kind=kOutput, calls=%fused_computation.18 | convolution fusion | flops 9405857792 | bytes 63120000 | tf_op jit(solution)/shard_map/ky,sckzl->scyzl/dot_general | solution.py:88
  1351.5 69.9 %fusion.3 = f32[2,320,32,128]{3,1,2,0:T(8,128)} fusion(f32[4,320,32,128]{3,1,2,0:T(8,128)} %fusion.59, f32[4,320,32,128]{3,1,2,0:T(8,128)} %fusion.56, f32[2,4,32,128,320]{3,4,2,1,0:T(8,128)} %fusion.90, f32[2,4,32,128,320]{3,4,2,1,0:T(8,128)} %fusion.13, s32[128]{0:T(128)S(1)} %iota_add_fusion, pred[128]{0:T(512)(128)(4,1)S(1)} %iota_compare_fusion.4), kind=kOutput, calls=%fused_computation.4 | convolution fusion | flops 16166551552 | bytes 136315520 | tf_op jit(solution)/shard_map/...l,lm->...m/dot_general | solution.py:39
  1421.4 14.0 copy.70
  1435.4 0.0 all-gather.3.cloned.1.call-update
  1435.4 251.0 %all-gather.3.cloned.1.call-done = f32[8,320,32,128]{3,2,1,0:T(8,128)} async-done(((f32[2,320,32,128]{3,2,1,0:T(8,128)}), f32[8,320,32,128]{3,2,1,0:T(8,128)}) %all-gather.3.cloned.1.call-update) | async-done | bytes 41943056 | tf_op jit(solution)/shard_map/all_gather | solution.py:102
  1686.4 19.5 %reduce_sum.19 = bf16[2,320,32,128]{3,2,1,0:T(8,128)(2,1)} reduce(f32[4,2,320,32,128]{4,3,2,1,0:T(8,128)} %bitcast.177, f32[]{:T(128)} %constant.63.clone.1), dimensions={0}, to_apply=%region_1.2 | reduce | flops 7864320 | bytes 47185924 | tf_op jit(solution)/shard_map/reduce_sum | solution.py:102
  1705.9 2.6 dynamic-slice_convert_fusion
  (7 shorter events, 0.0 us)
Async XLA Ops:
  6.5 19.0 %slice-start = ((s8[10485760]{0:T(1024)(128)(4,1)}), s8[4194304]{0:T(1024)(128)(4,1)S(1)}, s32[]{:S(2)}) async-start(s8[10485760]{0:T(1024)(128)(4,1)} %bitcast.175), calls=%async_computation.3 | async-start | bytes 8388608
  8.5 17.0 slice-start.1
  16.9 8.6 slice-start.2
  152.9 460.0 %all-to-all-start = ((bf16[2,4,320,32,128]{4,3,1,0,2:T(8,128)(2,1)}), bf16[2,4,320,32,128]{4,3,1,0,2:T(8,128)(2,1)}, u32[]{:S(2)}, u32[]{:S(2)}) async-start(bf16[2,4,320,32,128]{4,3,1,0,2:T(8,128)(2,1)} %copy.55), calls=%async_computation | async-start | bytes 41943040 | tf_op jit(solution)/shard_map/all_to_all | solution.py:99
  159.7 15.8 copy-start
  820.5 457.5 %all-to-all-start.1 = ((bf16[2,4,40,256,128]{4,2,1,0,3:T(8,128)(2,1)}), bf16[2,4,40,256,128]{4,2,1,0,3:T(8,128)(2,1)}, u32[]{:S(2)}, u32[]{:S(2)}) async-start(bf16[2,4,40,256,128]{4,2,1,0,3:T(8,128)(2,1)} %copy.65), calls=%async_computation.1 | async-start | bytes 41943040 | tf_op jit(solution)/shard_map/all_to_all | solution.py:100
  826.6 859.8 %all-gather.3.cloned.1.call-start = ((), (), s32[]{:S(2)}) async-start(), calls=%async_computation.2 | async-start | bytes 52428800 | tf_op jit(solution)/shard_map/all_gather | solution.py:102
Sparse Core Ops, SparseCore 0:
  1435.5 250.8 all-gather.2
